TPU v7x, 256 devices: a whole 4x4x8 slice. The times are simulated.
256 devices in a mesh: band: 16 (over z, x_hi), domain: 16 (over y, x_lo, core).
Axes of the slice: x: 4 (x_hi: 2, x_lo: 2; x = x_hi * 2 + x_lo), y: 4, z: 8, core: 2. Of those that a mesh axis runs over, the one named last changes fastest.
Arguments:
- orbitals: float32 [256, 16384], P('band', 'domain'), may hold values from -12 to 12
- potential: float32 [16384], P('domain'), may hold values from -9 to 4.5
- stencil: int32 [36, 16384], P(None, 'domain'), may hold values from 0 to 1536, as said below
- send_list: int32 [2, 4096], P(None, 'domain'), may hold values from 0 to 1023, as said below
- send_count: int32 [2, 16], P(None, 'domain'), may hold values from 0 to 256, as said below
Outputs:
- filtered: float32 [256, 16384], P('band', 'domain')
- correlation: float32 [256, 256], P('band', 'domain')
- subspace: float32 [256, 256], P('band', 'domain')
Inputs may be any that keep to these rules, and one draw needn't show every extreme that they name: `stencil`: entries below 1024 name a slot of the point's own subdomain; entries from 1024 on name only live boundary rows of an existing neighbouring subdomain; 1536 marks a neighbour outside the cluster. `send_list`: each list of 256 entries holds distinct slots of the sending subdomain. `send_count`: row 0 counts the rows subdomain d sends to d + 1, row 1 those it sends to d - 1; zero toward a missing neighbour; 256 is reached in every draw.
All inputs are finite; a program needn't handle non-finite values.
Results may differ from a plain program's by a relative error of at most 0.00015.
Values sent between devices are 32-bit elements; how exact they have to be, the bound alone decides.
No kernel may reach another device: no remote copies, remote signals or barrier semaphores. Data moves between devices by JAX's collectives and lax.ppermute only.
A program may use at most 128 MiB of HBM per device.

v0:
```python
import jax
import jax.numpy as jnp
from jax import lax
from jax.sharding import PartitionSpec as P

DEGREE = 4
WEIGHTS = (
    -5369.0 / 1800.0,
    12.0 / 7.0,
    -15.0 / 56.0,
    10.0 / 189.0,
    -1.0 / 112.0,
    2.0 / 1925.0,
    -1.0 / 16632.0,
)
KINETIC = 50.0 / 9.0
CUT_SHARE = 0.1
SPECTRAL_REACH = (
    KINETIC
    * 3.0
    * (
        abs(WEIGHTS[0])
        + 2.0
        * (
            abs(WEIGHTS[1])
            + abs(WEIGHTS[2])
            + abs(WEIGHTS[3])
            + abs(WEIGHTS[4])
            + abs(WEIGHTS[5])
            + abs(WEIGHTS[6])
        )
    )
)


def with_halo(block, sides, width):
    for axis, dim in sides:
        count = lax.axis_size(axis)
        forward = [(i, i + 1) for i in range(count - 1)]
        backward = [(target, source) for source, target in forward]
        low = lax.ppermute(
            lax.slice_in_dim(block, block.shape[dim] - width, None, axis=dim), axis, forward
        )
        high = lax.ppermute(lax.slice_in_dim(block, 0, width, axis=dim), axis, backward)
        block = jnp.concatenate([low, block, high], axis=dim)
    return block


def apply_operator(values, potential, stencil, send_list, live_slots):
    capacity = send_list.shape[1]
    sent_rows = values[:, send_list]
    sent_rows = jnp.where(live_slots[None], sent_rows, jnp.zeros_like(sent_rows))
    outgoing = jnp.concatenate([sent_rows[:, 1], sent_rows[:, 0]], axis=1)
    padded = with_halo(outgoing, (("domain", 1),), capacity)
    from_below = padded[:, :capacity]
    from_above = padded[:, 3 * capacity :]
    zero_column = jnp.zeros((values.shape[0], 1), values.dtype)
    buffer = jnp.concatenate([values, from_below, from_above, zero_column], axis=1)
    near_sum = jnp.zeros_like(values)
    for distance in range(6):
        cycle_sum = jnp.zeros_like(values)
        for member in range(6):
            cycle_sum = cycle_sum + buffer[:, stencil[6 * distance + member]]
        near_sum = near_sum + WEIGHTS[distance + 1] * cycle_sum
    return potential * values - KINETIC * (3.0 * WEIGHTS[0] * values + near_sum)


def filter_block(orbitals, operator_fn, lowest, highest):
    top_bound = highest + SPECTRAL_REACH
    cut_point = lowest + CUT_SHARE * (top_bound - lowest)
    half_width = (top_bound - cut_point) / 2.0
    centre = (top_bound + cut_point) / 2.0
    sigma_now = half_width / (lowest - centre)
    sigma_scale = 2.0 / sigma_now
    previous = orbitals
    current = sigma_now / half_width * (operator_fn(orbitals) - centre * orbitals)
    for order_index in range(2, DEGREE + 1):
        sigma_next = 1.0 / (sigma_scale - sigma_now)
        following = (
            2.0 * sigma_next / half_width * (operator_fn(current) - centre * current)
            - sigma_now * sigma_next * previous
        )
        previous = current
        current = following
        sigma_now = sigma_next
    return current


def inner_products(left_block, right_block):
    return lax.dot_general(
        left_block,
        right_block,
        (((1,), (1,)), ((), ())),
        precision=lax.Precision.HIGHEST,
        preferred_element_type=jnp.float32,
    )


def shards(orbitals, potential, stencil, send_list, send_count):
    points = orbitals.shape[1]
    capacity = send_list.shape[1]
    domain_count = lax.axis_size("domain")
    total_points = points * domain_count
    lowest = lax.pmin(jnp.min(potential), "domain")
    highest = lax.pmax(jnp.max(potential), "domain")
    live_slots = lax.broadcasted_iota(jnp.int32, (2, capacity), 1) < send_count

    def operator_fn(values):
        return apply_operator(values, potential, stencil, send_list, live_slots)

    filtered = filter_block(orbitals, operator_fn, lowest, highest)
    applied = operator_fn(filtered)
    piece_values = lax.all_gather(filtered, "band", axis=0, tiled=True)
    piece_applied = lax.all_gather(applied, "band", axis=0, tiled=True)
    correlation_part = inner_products(filtered, piece_values)
    subspace_part = inner_products(filtered, piece_applied)
    correlation_part, subspace_part = (correlation_part, subspace_part)
    correlation_sum, subspace_sum = (
        lax.psum_scatter(correlation_part, "domain", scatter_dimension=1, tiled=True),
        lax.psum_scatter(subspace_part, "domain", scatter_dimension=1, tiled=True),
    )
    return (filtered, correlation_sum / total_points, subspace_sum / total_points)


def solution(mesh):
    placed = (
        P("band", "domain"),
        P("domain"),
        P(None, "domain"),
        P(None, "domain"),
        P(None, "domain"),
    )
    return jax.shard_map(
        shards,
        mesh=mesh,
        in_specs=placed,
        out_specs=(P("band", "domain"), P("band", "domain"), P("band", "domain")),
        check_vma=False,
    )
```

profile of v0, /device:TPU:4, one launch (start us, length us, event | category | flops | bytes accessed | tf_op | source)
XLA Modules:
  0.0 1158.1 jit_solution(5905052475874954502)
XLA Ops:
  16.9 32.3 %pmax.7 = f32[]{:T(128)} all-reduce(f32[]{:T(128)} %get-tuple-element.19), channel_id=1, replica_groups=mesh['band'=16,'domain'=16] {'domain'}, use_global_device_ids=true, to_apply=%region_3.0 | all-reduce | flops 1 | bytes 8 | tf_op jit(solution)/shard_map/pmax | solution.py:105
  49.2 27.8 %pmin.7 = f32[]{:T(128)} all-reduce(f32[]{:T(128)} %get-tuple-element.18), channel_id=1, replica_groups=mesh['band'=16,'domain'=16] {'domain'}, use_global_device_ids=true, to_apply=%region_1.0 | all-reduce | flops 1 | bytes 8 | tf_op jit(solution)/shard_map/pmin | solution.py:104
  209.8 4.0 gather_fusion.56
  233.7 4.0 gather_fusion.62
  237.7 4.0 gather_fusion.63
  257.7 4.0 gather_fusion.68
  261.7 4.0 gather_fusion.69
  269.7 4.0 gather_fusion.71
  301.6 4.0 gather_fusion.46
  405.6 4.0 gather_fusion.93
  429.6 4.0 gather_fusion.99
  433.6 4.0 gather_fusion.100
  453.5 4.0 gather_fusion.105
  457.5 4.0 gather_fusion.106
  465.5 4.0 gather_fusion.108
  497.5 4.0 gather_fusion.83
  601.5 4.0 gather_fusion.130
  617.4 4.0 gather_fusion.134
  645.4 4.0 gather_fusion.141
  657.4 4.0 gather_fusion.144
  661.4 4.0 gather_fusion.145
  697.3 4.0 gather_fusion.121
  804.8 4.0 gather_fusion.171
  836.8 4.0 gather_fusion.179
  844.8 4.0 gather_fusion.181
  856.7 4.0 gather_fusion.151
  876.7 4.0 gather_fusion.156
  896.7 4.0 gather_fusion.161
  908.7 4.0 gather_fusion.164
  944.3 76.7 %all-gather.5.cloned.1.call-done = f32[256,1024]{1,0:T(8,128)} async-done(((f32[16,1024]{1,0:T(8,128)}), f32[256,1024]{1,0:T(8,128)}) %all-gather.5.cloned.1.call-update) | async-done | bytes 1048592 | tf_op jit(solution)/shard_map/all_gather | solution.py:114
  1023.9 61.8 %reduce-scatter.7.cloned.1.call-done = f32[16,16]{1,0:T(8,128)} async-done(((f32[256,16]{1,0:T(8,128)}), f32[16,16]{1,0:T(8,128)}) %reduce-scatter.7.cloned.1.call-update) | async-done | bytes 1040
  1087.1 62.9 %reduce-scatter.9.cloned.1.call-done = f32[16,16]{1,0:T(8,128)} async-done(((f32[256,16]{1,0:T(8,128)}), f32[16,16]{1,0:T(8,128)}) %reduce-scatter.9.cloned.1.call-update) | async-done | bytes 1040
  (1131 shorter events, 769.2 us)
Async XLA Ops:
  7.2 934.3 %all-gather.3.cloned.1.call-start = ((), (), s32[]{:S(2)}) async-start(), calls=%async_computation.2 | async-start | bytes 1114112 | tf_op jit(solution)/shard_map/all_gather | solution.py:113
  11.4 68.0 %collective-permute-start = (f32[16,256]{1,0:T(8,128)S(1)}, f32[16,256]{1,0:T(8,128)S(1)}, u32[]{:S(2)}, u32[]{:S(2)}) collective-permute-start(f32[16,256]{1,0:T(8,128)S(1)} %get-tuple-element.64), channel_id=1, source_target_pairs={{0,1},{1,2},{2,3},{3,4},{4,5},{5,6},{6,7},{7,8},{8,9},{9,10},{10,1... | collective-permute-start | bytes 49160 | tf_op jit(solution)/shard_map/ppermute | solution.py:41
  13.2 66.4 %collective-permute-start.1 = (f32[16,256]{1,0:T(8,128)S(1)}, f32[16,256]{1,0:T(8,128)S(1)}, u32[]{:S(2)}, u32[]{:S(2)}) collective-permute-start(f32[16,256]{1,0:T(8,128)S(1)} %get-tuple-element.65), channel_id=1, source_target_pairs={{1,0},{2,1},{3,2},{4,3},{5,4},{6,5},{7,6},{8,7},{9,8},{10,9},{11,1... | collective-permute-start | bytes 49160 | tf_op jit(solution)/shard_map/ppermute | solution.py:44
  15.1 118.7 %copy-start.239 = (s32[1024]{0:T(1024)}, s32[1024]{0:T(1024)S(1)}, u32[]{:S(2)}) copy-start(s32[1024]{0:T(1024)S(1)} %broadcast_clamp_fusion.2) | copy-start | bytes 12292
  15.1 121.6 %copy-start.244 = (s32[1024]{0:T(1024)}, s32[1024]{0:T(1024)S(1)}, u32[]{:S(2)}) copy-start(s32[1024]{0:T(1024)S(1)} %broadcast_clamp_fusion.35) | copy-start | bytes 12292
  15.2 124.6 %copy-start.249 = (s32[1024]{0:T(1024)}, s32[1024]{0:T(1024)S(1)}, u32[]{:S(2)}) copy-start(s32[1024]{0:T(1024)S(1)} %broadcast_clamp_fusion.33) | copy-start | bytes 12292
  15.2 127.6 %copy-start.254 = (s32[1024]{0:T(1024)}, s32[1024]{0:T(1024)S(1)}, u32[]{:S(2)}) copy-start(s32[1024]{0:T(1024)S(1)} %broadcast_clamp_fusion.32) | copy-start | bytes 12292
  15.2 130.5 %copy-start.259 = (s32[1024]{0:T(1024)}, s32[1024]{0:T(1024)S(1)}, u32[]{:S(2)}) copy-start(s32[1024]{0:T(1024)S(1)} %broadcast_clamp_fusion.31) | copy-start | bytes 12292
  15.2 133.5 %copy-start.264 = (s32[1024]{0:T(1024)}, s32[1024]{0:T(1024)S(1)}, u32[]{:S(2)}) copy-start(s32[1024]{0:T(1024)S(1)} %broadcast_clamp_fusion.30) | copy-start | bytes 12292
  15.3 136.5 %copy-start.269 = (s32[1024]{0:T(1024)}, s32[1024]{0:T(1024)S(1)}, u32[]{:S(2)}) copy-start(s32[1024]{0:T(1024)S(1)} %broadcast_clamp_fusion.29) | copy-start | bytes 12292
  15.3 139.4 %copy-start.274 = (s32[1024]{0:T(1024)}, s32[1024]{0:T(1024)S(1)}, u32[]{:S(2)}) copy-start(s32[1024]{0:T(1024)S(1)} %broadcast_clamp_fusion.28) | copy-start | bytes 12292
  15.3 142.4 %copy-start.279 = (s32[1024]{0:T(1024)}, s32[1024]{0:T(1024)S(1)}, u32[]{:S(2)}) copy-start(s32[1024]{0:T(1024)S(1)} %broadcast_clamp_fusion.27) | copy-start | bytes 12292
  15.3 145.4 %copy-start.284 = (s32[1024]{0:T(1024)}, s32[1024]{0:T(1024)S(1)}, u32[]{:S(2)}) copy-start(s32[1024]{0:T(1024)S(1)} %broadcast_clamp_fusion.26) | copy-start | bytes 12292
  15.4 148.3 %copy-start.289 = (s32[1024]{0:T(1024)}, s32[1024]{0:T(1024)S(1)}, u32[]{:S(2)}) copy-start(s32[1024]{0:T(1024)S(1)} %broadcast_clamp_fusion.25) | copy-start | bytes 12292
  15.4 151.3 %copy-start.294 = (s32[1024]{0:T(1024)}, s32[1024]{0:T(1024)S(1)}, u32[]{:S(2)}) copy-start(s32[1024]{0:T(1024)S(1)} %broadcast_clamp_fusion.24) | copy-start | bytes 12292
  15.4 154.3 %copy-start.299 = (s32[1024]{0:T(1024)}, s32[1024]{0:T(1024)S(1)}, u32[]{:S(2)}) copy-start(s32[1024]{0:T(1024)S(1)} %broadcast_clamp_fusion.23) | copy-start | bytes 12292
  15.4 157.2 %copy-start.304 = (s32[1024]{0:T(1024)}, s32[1024]{0:T(1024)S(1)}, u32[]{:S(2)}) copy-start(s32[1024]{0:T(1024)S(1)} %broadcast_clamp_fusion.22) | copy-start | bytes 12292
  15.4 160.2 %copy-start.309 = (s32[1024]{0:T(1024)}, s32[1024]{0:T(1024)S(1)}, u32[]{:S(2)}) copy-start(s32[1024]{0:T(1024)S(1)} %broadcast_clamp_fusion.21) | copy-start | bytes 12292
  15.5 163.2 %copy-start.314 = (s32[1024]{0:T(1024)}, s32[1024]{0:T(1024)S(1)}, u32[]{:S(2)}) copy-start(s32[1024]{0:T(1024)S(1)} %broadcast_clamp_fusion.20) | copy-start | bytes 12292
  15.5 166.8 %copy-start.319 = (s32[1024]{0:T(1024)}, s32[1024]{0:T(1024)S(1)}, u32[]{:S(2)}) copy-start(s32[1024]{0:T(1024)S(1)} %broadcast_clamp_fusion.1) | copy-start | bytes 12292
  16.2 169.7 %copy-start.324 = (s32[1024]{0:T(1024)}, s32[1024]{0:T(1024)S(1)}, u32[]{:S(2)}) copy-start(s32[1024]{0:T(1024)S(1)} %broadcast_clamp_fusion) | copy-start | bytes 12292
  192.2 3.4 collective-permute-start.2
  194.0 3.1 collective-permute-start.3
  385.9 5.5 collective-permute-start.4
  389.9 3.1 collective-permute-start.5
  581.8 5.7 collective-permute-start.6
  585.7 3.1 collective-permute-start.7
  772.2 248.8 %all-gather.5.cloned.1.call-start = ((), (), s32[]{:S(2)}) async-start(), calls=%async_computation.3 | async-start | bytes 1114112 | tf_op jit(solution)/shard_map/all_gather | solution.py:114
  775.0 5.4 collective-permute-start.8
  778.9 3.1 collective-permute-start.9
  941.4 144.4 %reduce-scatter.7.cloned.1.call-start = ((), (), s32[]{:S(2)}) async-start(), calls=%async_computation.4 | async-start | bytes 139264
  944.3 205.8 %reduce-scatter.9.cloned.1.call-start = ((), (), s32[]{:S(2)}) async-start(), calls=%async_computation.5 | async-start | bytes 139264
  (321 other events, 2403.8 us)
Sparse Core Ops, SparseCore 0:
  772.3 78.6 all-gather.2
  941.5 79.5 all-gather.4
  1023.6 62.1 reduce-scatter.6
  1088.1 61.9 reduce-scatter.8
where the time goes:
time: 1170 us; the launch traced here: 1160 us
  local copies, waits for them, and re-layouts  837 us (72%)
  waiting for transfers between devices  207 us (18%)
  blocking collectives  60.1 us (5%)
  starting transfers between devices  22.8 us (2%)
  between operations  19.4 us (2%)
    gather x360, local copies, waits for them, and re-layouts, apply_operator(): cycle_sum = cycle_sum + buffer[:, stencil[6 * distance + member]]  804 us
    unnamed x6, waiting for transfers between devices  125 us
    all_gather x1, waiting for transfers between devices, shards(): piece_applied = lax.all_gather(applied, 'band', axis=0, tiled=True)  76.7 us
    pmax x1, blocking collectives, shards(): highest = lax.pmax(jnp.max(potential), 'domain')  32.3 us
    pmin x1, blocking collectives, shards(): lowest = lax.pmin(jnp.min(potential), 'domain')  27.8 us
    unnamed x682, local copies, waits for them, and re-layouts  25.6 us
  transfers between devices with their start and end apart: 14, of which 7 were waited for; matrix products, arithmetic and copies ran while one was open for 14% of the time, Pallas kernels for 0%

commit v1 on v0

--- a/solution.py
+++ b/solution.py
@@ -111,7 +111,9 @@
     filtered = filter_block(orbitals, operator_fn, lowest, highest)
     applied = operator_fn(filtered)
     piece_values = lax.all_gather(filtered, "band", axis=0, tiled=True)
-    piece_applied = lax.all_gather(applied, "band", axis=0, tiled=True)
+    piece_applied = jnp.concatenate(
+        lax.all_to_all(jnp.stack([applied] * lax.axis_size("band")), "band", 0, 0), axis=0
+    )
     correlation_part = inner_products(filtered, piece_values)
     subspace_part = inner_products(filtered, piece_applied)
     correlation_part, subspace_part = (correlation_part, subspace_part)

time: 1170 us -> 1110 us (0.949)
  waiting for transfers between devices: 207 us -> 134 us
    all_gather x1 -> x0, waiting for transfers between devices: 76.7 us -> none  [shards(): piece_applied = lax.all_gather(applied, 'band', axis=0, tiled=True)]
    all_to_all x0 -> x1, waiting for transfers between devices: none -> 22.9 us  [shards(): lax.all_to_all(jnp.stack([applied] * lax.axis_size('band')), 'band', 0, 0)]
    unnamed x6 -> x5, waiting for transfers between devices: 125 us -> 105 us
    unnamed x682 -> x686, local copies, waits for them, and re-layouts: 25.6 us -> 25.4 us
where the time goes in v1:
time: 1110 us; the launch traced here: 1100 us
  local copies, waits for them, and re-layouts  844 us (76%)
  waiting for transfers between devices  134 us (12%)
  blocking collectives  60.1 us (5%)
  starting transfers between devices  34.3 us (3%)
  between operations  19.5 us (2%)
    gather x360, local copies, waits for them, and re-layouts, apply_operator(): cycle_sum = cycle_sum + buffer[:, stencil[6 * distance + member]]  810 us
    unnamed x5, waiting for transfers between devices  105 us
    pmax x1, blocking collectives, shards(): highest = lax.pmax(jnp.max(potential), 'domain')  32.4 us
    pmin x1, blocking collectives, shards(): lowest = lax.pmin(jnp.min(potential), 'domain')  27.8 us
    unnamed x686, local copies, waits for them, and re-layouts  25.4 us
    all_to_all x1, waiting for transfers between devices, shards(): lax.all_to_all(jnp.stack([applied] * lax.axis_size('band')), 'band', 0, 0)  22.9 us
  transfers between devices with their start and end apart: 14, of which 7 were waited for; matrix products, arithmetic and copies ran while one was open for 14% of the time, Pallas kernels for 0%

profile of v1, /device:TPU:4, one launch (start us, length us, event | category | flops | bytes accessed | tf_op | source)
XLA Modules:
  0.0 1100.3 jit_solution(12916155106275560654)
XLA Ops:
  16.8 32.4 %pmax.7 = f32[]{:T(128)} all-reduce(f32[]{:T(128)} %get-tuple-element.19), channel_id=1, replica_groups=mesh['band'=16,'domain'=16] {'domain'}, use_global_device_ids=true, to_apply=%region_3.0 | all-reduce | flops 1 | bytes 8 | tf_op jit(solution)/shard_map/pmax | solution.py:105
  49.2 27.8 %pmin.7 = f32[]{:T(128)} all-reduce(f32[]{:T(128)} %get-tuple-element.18), channel_id=1, replica_groups=mesh['band'=16,'domain'=16] {'domain'}, use_global_device_ids=true, to_apply=%region_1.0 | all-reduce | flops 1 | bytes 8 | tf_op jit(solution)/shard_map/pmin | solution.py:104
  238.1 4.0 gather_fusion.63
  262.3 4.0 gather_fusion.69
  266.3 4.1 gather_fusion.70
  274.4 4.0 gather_fusion.38
  310.6 4.0 gather_fusion.48
  314.7 4.0 gather_fusion.49
  435.3 4.0 gather_fusion.100
  459.5 4.0 gather_fusion.106
  463.5 4.1 gather_fusion.107
  471.6 4.0 gather_fusion.75
  507.8 4.0 gather_fusion.85
  511.9 4.0 gather_fusion.86
  592.2 4.0 gather_fusion.113
  636.5 4.0 gather_fusion.138
  660.7 4.0 gather_fusion.144
  668.8 4.1 gather_fusion.112
  672.9 4.0 gather_fusion.114
  709.1 4.0 gather_fusion.123
  713.1 4.0 gather_fusion.124
  778.7 4.0 collective-permute-start.8
  800.7 4.0 gather_fusion.169
  837.0 4.0 gather_fusion.178
  845.0 4.1 gather_fusion.180
  849.1 4.0 gather_fusion.181
  873.3 4.0 gather_fusion.154
  901.5 4.0 gather_fusion.161
  946.8 11.4 %all-to-all-start = ((f32[16,16,1024]{2,1,0:T(8,128)}), f32[16,16,1024]{2,1,0:T(8,128)S(1)}, u32[]{:S(2)}, u32[]{:S(2)}) async-start(f32[16,16,1024]{2,1,0:T(8,128)} %stack.2), calls=%async_computation | async-start | bytes 2097152 | tf_op jit(solution)/shard_map/all_to_all | solution.py:115
  961.3 22.9 %all-to-all-done = f32[16,16,1024]{2,1,0:T(8,128)S(1)} async-done(((f32[16,16,1024]{2,1,0:T(8,128)}), f32[16,16,1024]{2,1,0:T(8,128)S(1)}, u32[]{:S(2)}, u32[]{:S(2)}) %all-to-all-start) | async-done | bytes 1048608 | tf_op jit(solution)/shard_map/all_to_all | solution.py:115
  985.8 40.2 %reduce-scatter.7.cloned.1.call-done = f32[16,16]{1,0:T(8,128)} async-done(((f32[256,16]{1,0:T(8,128)}), f32[16,16]{1,0:T(8,128)}) %reduce-scatter.7.cloned.1.call-update) | async-done | bytes 1040
  1027.3 64.9 %reduce-scatter.9.cloned.1.call-done = f32[16,16]{1,0:T(8,128)} async-done(((f32[256,16]{1,0:T(8,128)}), f32[16,16]{1,0:T(8,128)}) %reduce-scatter.9.cloned.1.call-update) | async-done | bytes 1040
  (1135 shorter events, 776.2 us)
Async XLA Ops:
  7.2 951.2 %all-gather.2.cloned.1.call-start = ((), (), s32[]{:S(2)}) async-start(), calls=%async_computation.3 | async-start | bytes 1114112 | tf_op jit(solution)/shard_map/all_gather | solution.py:113
  11.4 68.1 %collective-permute-start = (f32[16,256]{1,0:T(8,128)S(1)}, f32[16,256]{1,0:T(8,128)S(1)}, u32[]{:S(2)}, u32[]{:S(2)}) collective-permute-start(f32[16,256]{1,0:T(8,128)S(1)} %get-tuple-element.64), channel_id=1, source_target_pairs={{0,1},{1,2},{2,3},{3,4},{4,5},{5,6},{6,7},{7,8},{8,9},{9,10},{10,1... | collective-permute-start | bytes 49160 | tf_op jit(solution)/shard_map/ppermute | solution.py:41
  13.2 66.5 %collective-permute-start.1 = (f32[16,256]{1,0:T(8,128)S(1)}, f32[16,256]{1,0:T(8,128)S(1)}, u32[]{:S(2)}, u32[]{:S(2)}) collective-permute-start(f32[16,256]{1,0:T(8,128)S(1)} %get-tuple-element.65), channel_id=1, source_target_pairs={{1,0},{2,1},{3,2},{4,3},{5,4},{6,5},{7,6},{8,7},{9,8},{10,9},{11,1... | collective-permute-start | bytes 49160 | tf_op jit(solution)/shard_map/ppermute | solution.py:44
  15.1 118.7 %copy-start.241 = (s32[1024]{0:T(1024)}, s32[1024]{0:T(1024)S(1)}, u32[]{:S(2)}) copy-start(s32[1024]{0:T(1024)S(1)} %broadcast_clamp_fusion.2) | copy-start | bytes 12292
  15.2 121.7 %copy-start.246 = (s32[1024]{0:T(1024)}, s32[1024]{0:T(1024)S(1)}, u32[]{:S(2)}) copy-start(s32[1024]{0:T(1024)S(1)} %broadcast_clamp_fusion.35) | copy-start | bytes 12292
  15.2 124.6 %copy-start.251 = (s32[1024]{0:T(1024)}, s32[1024]{0:T(1024)S(1)}, u32[]{:S(2)}) copy-start(s32[1024]{0:T(1024)S(1)} %broadcast_clamp_fusion.33) | copy-start | bytes 12292
  15.2 127.6 %copy-start.256 = (s32[1024]{0:T(1024)}, s32[1024]{0:T(1024)S(1)}, u32[]{:S(2)}) copy-start(s32[1024]{0:T(1024)S(1)} %broadcast_clamp_fusion.32) | copy-start | bytes 12292
  15.2 130.6 %copy-start.261 = (s32[1024]{0:T(1024)}, s32[1024]{0:T(1024)S(1)}, u32[]{:S(2)}) copy-start(s32[1024]{0:T(1024)S(1)} %broadcast_clamp_fusion.31) | copy-start | bytes 12292
  15.2 133.5 %copy-start.266 = (s32[1024]{0:T(1024)}, s32[1024]{0:T(1024)S(1)}, u32[]{:S(2)}) copy-start(s32[1024]{0:T(1024)S(1)} %broadcast_clamp_fusion.30) | copy-start | bytes 12292
  15.3 136.5 %copy-start.271 = (s32[1024]{0:T(1024)}, s32[1024]{0:T(1024)S(1)}, u32[]{:S(2)}) copy-start(s32[1024]{0:T(1024)S(1)} %broadcast_clamp_fusion.29) | copy-start | bytes 12292
  15.3 139.5 %copy-start.276 = (s32[1024]{0:T(1024)}, s32[1024]{0:T(1024)S(1)}, u32[]{:S(2)}) copy-start(s32[1024]{0:T(1024)S(1)} %broadcast_clamp_fusion.28) | copy-start | bytes 12292
  15.3 142.4 %copy-start.281 = (s32[1024]{0:T(1024)}, s32[1024]{0:T(1024)S(1)}, u32[]{:S(2)}) copy-start(s32[1024]{0:T(1024)S(1)} %broadcast_clamp_fusion.27) | copy-start | bytes 12292
  15.3 145.4 %copy-start.286 = (s32[1024]{0:T(1024)}, s32[1024]{0:T(1024)S(1)}, u32[]{:S(2)}) copy-start(s32[1024]{0:T(1024)S(1)} %broadcast_clamp_fusion.26) | copy-start | bytes 12292
  15.4 148.4 %copy-start.291 = (s32[1024]{0:T(1024)}, s32[1024]{0:T(1024)S(1)}, u32[]{:S(2)}) copy-start(s32[1024]{0:T(1024)S(1)} %broadcast_clamp_fusion.25) | copy-start | bytes 12292
  15.4 151.3 %copy-start.296 = (s32[1024]{0:T(1024)}, s32[1024]{0:T(1024)S(1)}, u32[]{:S(2)}) copy-start(s32[1024]{0:T(1024)S(1)} %broadcast_clamp_fusion.24) | copy-start | bytes 12292
  15.4 154.3 %copy-start.301 = (s32[1024]{0:T(1024)}, s32[1024]{0:T(1024)S(1)}, u32[]{:S(2)}) copy-start(s32[1024]{0:T(1024)S(1)} %broadcast_clamp_fusion.23) | copy-start | bytes 12292
  15.4 157.3 %copy-start.306 = (s32[1024]{0:T(1024)}, s32[1024]{0:T(1024)S(1)}, u32[]{:S(2)}) copy-start(s32[1024]{0:T(1024)S(1)} %broadcast_clamp_fusion.22) | copy-start | bytes 12292
  15.4 160.2 %copy-start.311 = (s32[1024]{0:T(1024)}, s32[1024]{0:T(1024)S(1)}, u32[]{:S(2)}) copy-start(s32[1024]{0:T(1024)S(1)} %broadcast_clamp_fusion.21) | copy-start | bytes 12292
  15.5 163.2 %copy-start.316 = (s32[1024]{0:T(1024)}, s32[1024]{0:T(1024)S(1)}, u32[]{:S(2)}) copy-start(s32[1024]{0:T(1024)S(1)} %broadcast_clamp_fusion.20) | copy-start | bytes 12292
  15.5 166.8 %copy-start.321 = (s32[1024]{0:T(1024)}, s32[1024]{0:T(1024)S(1)}, u32[]{:S(2)}) copy-start(s32[1024]{0:T(1024)S(1)} %broadcast_clamp_fusion.1) | copy-start | bytes 12292
  16.2 169.7 %copy-start.326 = (s32[1024]{0:T(1024)}, s32[1024]{0:T(1024)S(1)}, u32[]{:S(2)}) copy-start(s32[1024]{0:T(1024)S(1)} %broadcast_clamp_fusion) | copy-start | bytes 12292
  192.3 3.4 collective-permute-start.2
  194.1 3.1 collective-permute-start.3
  387.4 5.5 collective-permute-start.4
  391.3 3.1 collective-permute-start.5
  584.6 5.7 collective-permute-start.6
  588.5 3.1 collective-permute-start.7
  778.7 5.5 collective-permute-start.8
  782.8 3.1 collective-permute-start.9
  946.8 37.3 %all-to-all-start = ((f32[16,16,1024]{2,1,0:T(8,128)}), f32[16,16,1024]{2,1,0:T(8,128)S(1)}, u32[]{:S(2)}, u32[]{:S(2)}) async-start(f32[16,16,1024]{2,1,0:T(8,128)} %stack.2), calls=%async_computation | async-start | bytes 2097152 | tf_op jit(solution)/shard_map/all_to_all | solution.py:115
  958.3 67.7 %reduce-scatter.7.cloned.1.call-start = ((), (), s32[]{:S(2)}) async-start(), calls=%async_computation.4 | async-start | bytes 139264
  961.2 131.0 %reduce-scatter.9.cloned.1.call-start = ((), (), s32[]{:S(2)}) async-start(), calls=%async_computation.5 | async-start | bytes 139264
  (323 other events, 2417.7 us)
Sparse Core Ops, SparseCore 0:
  784.4 78.6 all-gather.1
  961.6 64.3 reduce-scatter.6
  1028.4 63.7 reduce-scatter.8
